TPU v7x, 256 devices: a whole 4x4x8 slice. The times are simulated.
256 devices in a mesh: dp: 32 (over z, y), tensor: 8 (over x, core).
Axes of the slice: x: 4, y: 4, z: 8, core: 2. Of those that a mesh axis runs over, the one named last changes fastest.
Arguments:
- tokens: bfloat16 [4096, 4096], P('dp', 'tensor'), may hold values from -6 to 6
- grad_out: bfloat16 [4096, 4096], P('dp', 'tensor'), may hold values from -6 to 6
- gate_blocks: int32 [8, 32], P('tensor'), may hold values from -1 to 447, as said below
- gate_values: bfloat16 [8, 32, 128, 128], P('tensor'), may hold values from -0.375 to 0.375
- up_blocks: int32 [8, 32], P('tensor'), may hold values from -1 to 447, as said below
- up_values: bfloat16 [8, 32, 128, 128], P('tensor'), may hold values from -0.375 to 0.375
- down_blocks: int32 [8, 32], P('tensor'), may hold values from -1 to 447, as said below
- down_values: bfloat16 [8, 32, 128, 128], P('tensor'), may hold values from -0.1875 to 0.1875
Outputs:
- mixed: bfloat16 [4096, 4096], P('dp', 'tensor')
- grad_tokens: bfloat16 [4096, 4096], P('dp', 'tensor')
- grad_gate: float32 [8, 32, 128, 128], P('tensor', 'dp')
- grad_up: float32 [8, 32, 128, 128], P('tensor', 'dp')
- grad_down: float32 [8, 32, 128, 128], P('tensor', 'dp')
Inputs may be any that keep to these rules, and one draw needn't show every extreme that they name: `gate_blocks`: each row lists distinct block numbers of one tensor shard in its first slots and -1 in the rest; a row has 16 to 32 listed blocks, one row has exactly 32 and another exactly 16. `up_blocks`: as for gate_blocks, drawn apart. `down_blocks`: as for gate_blocks, drawn apart.
All inputs are finite; a program needn't handle non-finite values.
Results may differ from a plain program's by a relative error of at most 0.015.
Values may be sent and summed in bfloat16 or wider, within the bound.
No kernel may reach another device: no remote copies, remote signals or barrier semaphores. Data moves between devices by JAX's collectives and lax.ppermute only.
A program may use at most 64 MiB of HBM per device.

v0:
```python
import jax
import jax.numpy as jnp
from jax import lax
from jax.sharding import PartitionSpec as P

FF = 14336


def locate(blocks, feature_count):
    flat = blocks[0]
    weight = (flat >= 0).astype(jnp.float32)
    safe = jnp.maximum(flat, 0)
    return (safe // feature_count, safe % feature_count, weight)


def one_hot(targets, weight, count):
    return (targets[:, None] == jnp.arange(count)[None, :]).astype(jnp.float32) * weight[:, None]


def spread(product, table):
    return jnp.einsum("tsn,sc->tcn", product, table, precision=lax.Precision.HIGHEST)


def select(source, position):
    return jnp.take(source, position, axis=1)


def forward_blocks(rows_in, values):
    return jnp.einsum("tsk,skn->tsn", rows_in, values, preferred_element_type=jnp.float32)


def backward_blocks(rows_in, values):
    return jnp.einsum("tsn,skn->tsk", rows_in, values, preferred_element_type=jnp.float32)


def slot_term(left, right, weight):
    product = jnp.einsum("tsk,tsn->skn", left, right, preferred_element_type=jnp.float32)
    return product * weight[:, None, None]


def body(
    tokens, grad_out, gate_blocks, gate_values, up_blocks, up_values, down_blocks, down_values
):
    gathered_x, gathered_dy = (
        lax.all_gather(tokens, "tensor", axis=1, tiled=True),
        lax.all_gather(grad_out, "tensor", axis=1, tiled=True),
    )
    tok_rows, feature_width = gathered_x.shape
    block_size = gate_values.shape[-1]
    feature_count = feature_width // block_size
    hidden_count = FF // (block_size * lax.axis_size("tensor"))
    inputs = gathered_x.reshape(tok_rows, feature_count, block_size)
    upstream = gathered_dy.reshape(tok_rows, feature_count, block_size)
    gate_hid, gate_feat, gate_live = locate(gate_blocks, feature_count)
    up_hid, up_feat, up_live = locate(up_blocks, feature_count)
    down_hid, down_feat, down_live = locate(down_blocks, feature_count)
    gate_rows = select(inputs, gate_feat)
    up_rows = select(inputs, up_feat)
    gate_pre = spread(
        forward_blocks(gate_rows, gate_values[0]), one_hot(gate_hid, gate_live, hidden_count)
    )
    up_pre = spread(forward_blocks(up_rows, up_values[0]), one_hot(up_hid, up_live, hidden_count))
    sigma_gate = jax.nn.sigmoid(gate_pre)
    activated = gate_pre * sigma_gate
    hidden = (activated * up_pre).astype(jnp.bfloat16)
    hidden_rows = select(hidden, down_hid)
    mixed_part = spread(
        forward_blocks(hidden_rows, down_values[0]), one_hot(down_feat, down_live, feature_count)
    )
    mixed_part = mixed_part.reshape(tok_rows, feature_width)
    upstream_rows = select(upstream, down_feat)
    mixed = lax.psum_scatter(
        mixed_part.astype(jnp.bfloat16), "tensor", scatter_dimension=1, tiled=True
    )
    hidden_grad = spread(
        backward_blocks(upstream_rows, down_values[0]), one_hot(down_hid, down_live, hidden_count)
    )
    gate_delta = (hidden_grad * up_pre * sigma_gate * (1.0 + gate_pre * (1.0 - sigma_gate))).astype(
        jnp.bfloat16
    )
    up_delta = (hidden_grad * activated).astype(jnp.bfloat16)
    gate_delta_rows = select(gate_delta, gate_hid)
    up_delta_rows = select(up_delta, up_hid)
    input_part = spread(
        backward_blocks(gate_delta_rows, gate_values[0]),
        one_hot(gate_feat, gate_live, feature_count),
    )
    input_part = input_part + spread(
        backward_blocks(up_delta_rows, up_values[0]), one_hot(up_feat, up_live, feature_count)
    )
    input_part = input_part.reshape(tok_rows, feature_width)
    gate_term = slot_term(gate_rows, gate_delta_rows, gate_live)
    up_term = slot_term(up_rows, up_delta_rows, up_live)
    down_term = slot_term(hidden_rows, upstream_rows, down_live)
    grad_gate, grad_up, grad_down = (
        lax.psum_scatter(term.astype(jnp.bfloat16), "dp", scatter_dimension=0, tiled=True).astype(
            jnp.float32
        )[None]
        for term in (gate_term, up_term, down_term)
    )
    grad_tokens = lax.psum_scatter(
        input_part.astype(jnp.bfloat16), "tensor", scatter_dimension=1, tiled=True
    )
    return (mixed, grad_tokens, grad_gate, grad_up, grad_down)


def solution(mesh):
    in_specs = (
        P("dp", "tensor"),
        P("dp", "tensor"),
        P("tensor", None),
        P("tensor", None, None, None),
        P("tensor", None),
        P("tensor", None, None, None),
        P("tensor", None),
        P("tensor", None, None, None),
    )
    out_specs = (
        P("dp", "tensor"),
        P("dp", "tensor"),
        P("tensor", "dp", None, None),
        P("tensor", "dp", None, None),
        P("tensor", "dp", None, None),
    )
    return jax.shard_map(body, mesh=mesh, in_specs=in_specs, out_specs=out_specs, check_vma=False)
```

profile of v0, /device:TPU:8, one launch (start us, length us, event | category | flops | bytes accessed | tf_op | source)
XLA Modules:
  0.0 825.7 jit_solution(16852433310537458351)
XLA Ops:
  7.2 0.0 copy-start
  7.2 0.0 all-gather.3.cloned.1.call-start
  7.2 1.7 copy.39
  9.0 0.0 all-gather.3.cloned.1.call-update
  9.0 0.0 all-gather.5.cloned.1.call-start
  9.0 1.7 copy.47
  10.7 0.0 all-gather.5.cloned.1.call-update
  10.7 0.0 reduce-scatter.10.cloned.1.call-start
  10.8 0.7 compare_and_fusion
  11.5 0.7 compare_and_fusion.2
  12.2 0.7 compare_and_fusion.1
  12.9 0.7 fusion.78
  13.6 0.7 fusion.79
  14.2 0.7 fusion.77
  14.9 24.2 %all-gather.3.cloned.1.call-done = bf16[128,4096]{0,1:T(8,128)(2,1)} async-done(((bf16[128,512]{0,1:T(8,128)(2,1)}), bf16[128,4096]{0,1:T(8,128)(2,1)}) %all-gather.3.cloned.1.call-update) | async-done | bytes 1048592 | tf_op jit(solution)/shard_map/all_gather | solution.py:45
  39.1 1.6 copy.40
  40.7 26.5 %all-gather.5.cloned.1.call-done = bf16[128,4096]{0,1:T(8,128)(2,1)} async-done(((bf16[128,512]{0,1:T(8,128)(2,1)}), bf16[128,4096]{0,1:T(8,128)(2,1)}) %all-gather.5.cloned.1.call-update) | async-done | bytes 1048592 | tf_op jit(solution)/shard_map/all_gather | solution.py:46
  67.2 2.3 copy.48
  69.5 1.7 gather_fusion.1
  71.2 1.7 gather_fusion
  72.8 3.0 gather_fusion.3
  75.8 0.0 copy-done.2
  75.8 0.0 copy-done.8
  75.8 0.5 convolution_bitcast_fusion.5
  76.3 0.0 copy-start.1
  76.3 2.2 fusion.10
  78.6 0.5 convolution_bitcast_fusion.4
  79.1 2.2 fusion.8
  81.4 0.9 convolution_bitcast_fusion.2
  82.3 2.2 fusion.4
  84.5 1.1 fusion.37
  85.6 1.7 gather_fusion.4
  87.2 3.2 multiply_convert_fusion.2
  90.4 0.0 reduce-scatter.10.cloned.1.call-update
  90.5 0.2 reduce-scatter.14.cloned.1.call-start
  90.7 1.7 gather_fusion.2
  92.4 3.2 multiply_convert_fusion
  95.6 0.0 reduce-scatter.14.cloned.1.call-update
  95.6 0.0 reduce-scatter.12.cloned.1.call-start
  95.7 1.6 gather_fusion.5
  97.3 3.3 multiply_convert_fusion.1
  100.6 0.0 reduce-scatter.12.cloned.1.call-update
  100.6 0.0 reduce-scatter.6.cloned.1.call-start
  100.7 0.5 convolution_bitcast_fusion.3
  101.2 3.0 fusion.14
  104.2 1.4 copy.90
  105.6 0.0 reduce-scatter.6.cloned.1.call-update
  105.6 0.0 copy-start.3
  105.6 0.0 reduce-scatter.8.cloned.1.call-start
  105.7 2.3 convolution_bitcast_fusion
  108.0 0.0 copy-done.4
  108.0 0.9 convolution_bitcast_fusion.1
  108.9 3.0 fusion
  111.9 3.1 add_convert_fusion
  115.0 1.4 copy.89
  116.4 0.0 reduce-scatter.8.cloned.1.call-update
  116.5 190.5 %reduce-scatter.10.cloned.1.call-done = bf16[1,128,128]{2,1,0:T(8,128)(2,1)} async-done(((bf16[32,128,128]{2,1,0:T(8,128)(2,1)}), bf16[1,128,128]{2,1,0:T(8,128)(2,1)}) %reduce-scatter.10.cloned.1.call-update) | async-done | bytes 32784 | tf_op jit(solution)/shard_map/reduce_scatter | solution.py:96
  307.0 1.4 bitcast_convert_fusion.2
  308.4 217.8 %reduce-scatter.14.cloned.1.call-done = bf16[1,128,128]{2,1,0:T(8,128)(2,1)} async-done(((bf16[32,128,128]{2,1,0:T(8,128)(2,1)}), bf16[1,128,128]{2,1,0:T(8,128)(2,1)}) %reduce-scatter.14.cloned.1.call-update) | async-done | bytes 32784 | tf_op jit(solution)/shard_map/reduce_scatter | solution.py:96
  526.2 1.4 bitcast_convert_fusion
  527.6 217.8 %reduce-scatter.12.cloned.1.call-done = bf16[1,128,128]{2,1,0:T(8,128)(2,1)} async-done(((bf16[32,128,128]{2,1,0:T(8,128)(2,1)}), bf16[1,128,128]{2,1,0:T(8,128)(2,1)}) %reduce-scatter.12.cloned.1.call-update) | async-done | bytes 32784 | tf_op jit(solution)/shard_map/reduce_scatter | solution.py:96
  745.4 1.4 bitcast_convert_fusion.1
  746.8 35.4 %reduce-scatter.6.cloned.1.call-done = bf16[128,512]{1,0:T(8,128)(2,1)} async-done(((bf16[128,4096]{1,0:T(8,128)(2,1)}), bf16[128,512]{1,0:T(8,128)(2,1)}) %reduce-scatter.6.cloned.1.call-update) | async-done | bytes 131088 | tf_op jit(solution)/shard_map/reduce_scatter | solution.py:72
  782.2 36.7 %reduce-scatter.8.cloned.1.call-done = bf16[128,512]{1,0:T(8,128)(2,1)} async-done(((bf16[128,4096]{1,0:T(8,128)(2,1)}), bf16[128,512]{1,0:T(8,128)(2,1)}) %reduce-scatter.8.cloned.1.call-update) | async-done | bytes 131088 | tf_op jit(solution)/shard_map/reduce_scatter | solution.py:101
  (24 shorter events, 0.1 us)
Async XLA Ops:
  7.2 74.2 %copy-start = (bf16[1,32,128,128]{3,2,1,0:T(8,128)(2,1)S(1)}, bf16[1,32,128,128]{3,2,1,0:T(8,128)(2,1)}, u32[]{:S(2)}) copy-start(bf16[1,32,128,128]{3,2,1,0:T(8,128)(2,1)} %param.19) | copy-start | bytes 3145732
  7.2 31.9 %all-gather.3.cloned.1.call-start = ((), (), s32[]{:S(2)}) async-start(), calls=%async_computation.5 | async-start | bytes 1179648 | tf_op jit(solution)/shard_map/all_gather | solution.py:45
  9.0 58.3 %all-gather.5.cloned.1.call-start = ((), (), s32[]{:S(2)}) async-start(), calls=%async_computation.7 | async-start | bytes 1179648 | tf_op jit(solution)/shard_map/all_gather | solution.py:46
  10.7 296.2 %reduce-scatter.10.cloned.1.call-start = ((), (), s32[]{:S(2)}) async-start(), calls=%async_computation.9 | async-start | bytes 1081344 | tf_op jit(solution)/shard_map/reduce_scatter | solution.py:96
  71.2 4.6 copy-start.2
  72.8 3.0 copy-start.8
  76.3 2.3 copy-start.1
  76.3 2.3 copy-start.5
  79.1 2.3 copy-start.6
  90.5 435.7 %reduce-scatter.14.cloned.1.call-start = ((), (), s32[]{:S(2)}) async-start(), calls=%async_computation.11 | async-start | bytes 1081344 | tf_op jit(solution)/shard_map/reduce_scatter | solution.py:96
  95.6 649.8 %reduce-scatter.12.cloned.1.call-start = ((), (), s32[]{:S(2)}) async-start(), calls=%async_computation.10 | async-start | bytes 1081344 | tf_op jit(solution)/shard_map/reduce_scatter | solution.py:96
  97.3 3.4 copy-start.7
  100.6 681.5 %reduce-scatter.6.cloned.1.call-start = ((), (), s32[]{:S(2)}) async-start(), calls=%async_computation.6 | async-start | bytes 1179648 | tf_op jit(solution)/shard_map/reduce_scatter | solution.py:72
  105.6 2.3 copy-start.3
  105.6 713.2 %reduce-scatter.8.cloned.1.call-start = ((), (), s32[]{:S(2)}) async-start(), calls=%async_computation.8 | async-start | bytes 1179648 | tf_op jit(solution)/shard_map/reduce_scatter | solution.py:101
  105.7 2.3 copy-start.4
Sparse Core Ops, SparseCore 0:
  10.4 28.6 all-gather.2
  41.5 25.6 all-gather.4
  90.6 216.3 reduce-scatter.9
  310.6 215.4 reduce-scatter.13
  529.8 215.5 reduce-scatter.11
  748.4 33.7 reduce-scatter.5
  785.3 33.5 reduce-scatter.7
where the time goes:
time: 826 us
  waiting for transfers between devices  749 us (91%)
  matrix products  31 us (4%)
  local copies, waits for them, and re-layouts  21.4 us (3%)
  between operations  14.4 us (2%)
  other arithmetic  9.27 us (1%)
    reduce_scatter x3, waiting for transfers between devices, body(): lax.psum_scatter(term.astype(jnp.bfloat16), 'dp', scatter_dimension=0, ti...  626 us
    reduce_scatter x1, waiting for transfers between devices, body(): lax.psum_scatter(input_part.astype(jnp.bfloat16), 'tensor', scatter_dimen...  36.7 us
    reduce_scatter x1, waiting for transfers between devices, body(): lax.psum_scatter(mixed_part.astype(jnp.bfloat16), 'tensor', scatter_dimen...  35.4 us
    all_gather x1, waiting for transfers between devices, body(): lax.all_gather(grad_out, 'tensor', axis=1, tiled=True)  26.5 us
    all_gather x1, waiting for transfers between devices, body(): lax.all_gather(tokens, 'tensor', axis=1, tiled=True)  24.2 us
  transfers between devices with their start and end apart: 7, of which 7 were waited for; matrix products, arithmetic and copies ran while one was open for 4% of the time, Pallas kernels for 0%

commit v1 on v0

--- a/solution.py
+++ b/solution.py
@@ -41,9 +41,20 @@
 def body(
     tokens, grad_out, gate_blocks, gate_values, up_blocks, up_values, down_blocks, down_values
 ):
+
+    def _reach_strips_all(load, axis_name):
+        degree = lax.axis_size(axis_name)
+        pool = []
+        for q in tuple(range(load.ndim)):
+            pool.append(degree if q == 1 else 1)
+        field_out = jnp.tile(load, pool)
+        return lax.all_to_all(
+            field_out, split_axis=1, axis_name=axis_name, concat_axis=1, tiled=True
+        )
+
     gathered_x, gathered_dy = (
         lax.all_gather(tokens, "tensor", axis=1, tiled=True),
-        lax.all_gather(grad_out, "tensor", axis=1, tiled=True),
+        _reach_strips_all(grad_out, "tensor"),
     )
     tok_rows, feature_width = gathered_x.shape
     block_size = gate_values.shape[-1]

time: 826 us -> 794 us (0.961)
  waiting for transfers between devices: 749 us -> 717 us
    all_gather x1 -> x0, waiting for transfers between devices: 26.5 us -> none  [body(): lax.all_gather(grad_out, 'tensor', axis=1, tiled=True)]
    all_gather x1, waiting for transfers between devices: 24.2 us -> 1.47 us  [body(): lax.all_gather(tokens, 'tensor', axis=1, tiled=True)]
    all_to_all x0 -> x1, waiting for transfers between devices: none -> 17.7 us  [_reach_strips_all(): lax.all_to_all(field_out, split_axis=1, axis_name=axis_name, concat_axis=...]
  transfers between devices with their start and end apart: 7 -> 7, of which waited for: 7 -> 7; matrix products, arithmetic and copies ran while one was open for 4% -> 5% of each run, Pallas kernels for 0% -> 0%
where the time goes in v1:
time: 794 us; the launch traced here: 793 us
  waiting for transfers between devices  717 us (90%)
  matrix products  33.3 us (4%)
  local copies, waits for them, and re-layouts  18.1 us (2%)
  between operations  14.5 us (2%)
    reduce_scatter x3, waiting for transfers between devices, body(): lax.psum_scatter(term.astype(jnp.bfloat16), 'dp', scatter_dimension=0, ti...  626 us
    reduce_scatter x1, waiting for transfers between devices, body(): lax.psum_scatter(input_part.astype(jnp.bfloat16), 'tensor', scatter_dimen...  36.6 us
    reduce_scatter x1, waiting for transfers between devices, body(): lax.psum_scatter(mixed_part.astype(jnp.bfloat16), 'tensor', scatter_dimen...  35.5 us
    all_to_all x1, waiting for transfers between devices, _reach_strips_all(): lax.all_to_all(field_out, split_axis=1, axis_name=axis_name, concat_axis=...  17.7 us
    dot_general x6, matrix products, spread(): jnp.einsum('tsn,sc->tcn', product, table, precision=lax.Precision.HIGHEST)  16.9 us
  transfers between devices with their start and end apart: 7, of which 7 were waited for; matrix products, arithmetic and copies ran while one was open for 5% of the time, Pallas kernels for 0%

profile of v1, /device:TPU:8, one launch (start us, length us, event | category | flops | bytes accessed | tf_op | source)
XLA Modules:
  0.0 793.3 jit_solution(9133521635743969930)
XLA Ops:
  7.2 0.0 copy-start
  7.2 0.0 copy-start.9
  7.2 0.0 copy-start.10
  7.2 0.0 copy-start.11
  7.2 0.0 all-gather.2.cloned.1.call-start
  7.3 1.7 copy.39
  9.0 0.0 all-gather.2.cloned.1.call-update
  9.0 1.0 copy.47
  10.0 1.1 tile.2
  11.2 4.3 all-to-all-start
  15.5 0.0 reduce-scatter.10.cloned.1.call-start
  15.5 0.0 copy-done.9
  15.6 0.0 copy-done.11
  15.7 17.7 %all-to-all-done = bf16[128,8,512]{0,2,1:T(8,128)(2,1)S(1)} async-done(((bf16[128,8,512]{0,2,1:T(8,128)(2,1)}), bf16[128,8,512]{0,2,1:T(8,128)(2,1)S(1)}, u32[]{:S(2)}, u32[]{:S(2)}) %all-to-all-start) | async-done | bytes 1048608 | tf_op jit(solution)/shard_map/all_to_all | solution.py:51
  33.4 0.7 copy.48
  34.1 0.7 gather_fusion.3
  34.9 0.9 convolution_bitcast_fusion.2
  35.8 0.1 copy-done.6
  35.8 3.2 fusion.4
  39.0 1.5 all-gather.2.cloned.1.call-done
  40.5 1.6 copy.40
  42.1 0.0 copy-start.2
  42.1 1.6 gather_fusion.1
  43.8 1.7 gather_fusion
  45.4 0.0 copy-done.2
  45.4 1.7 convolution_bitcast_fusion.5
  47.2 0.0 copy-start.1
  47.2 2.2 fusion.10
  49.5 0.5 convolution_bitcast_fusion.4
  50.0 2.2 fusion.8
  52.2 1.1 fusion.37
  53.3 1.7 gather_fusion.4
  55.0 3.2 multiply_convert_fusion.2
  58.1 0.0 reduce-scatter.10.cloned.1.call-update
  58.2 0.2 reduce-scatter.14.cloned.1.call-start
  58.4 1.7 gather_fusion.2
  60.1 3.2 multiply_convert_fusion
  63.3 0.0 reduce-scatter.14.cloned.1.call-update
  63.3 0.0 reduce-scatter.12.cloned.1.call-start
  63.4 1.7 gather_fusion.5
  65.0 3.3 multiply_convert_fusion.1
  68.3 0.0 reduce-scatter.12.cloned.1.call-update
  68.4 0.0 reduce-scatter.6.cloned.1.call-start
  68.4 0.5 convolution_bitcast_fusion.3
  68.9 3.0 fusion.14
  71.9 1.4 copy.90
  73.4 0.0 reduce-scatter.6.cloned.1.call-update
  73.4 0.0 copy-start.3
  73.4 0.0 reduce-scatter.8.cloned.1.call-start
  73.4 0.0 copy-start.4
  73.4 2.2 convolution_bitcast_fusion
  75.7 0.9 convolution_bitcast_fusion.1
  76.6 3.0 fusion
  79.6 3.1 add_convert_fusion
  82.8 1.4 copy.89
  84.2 0.0 reduce-scatter.8.cloned.1.call-update
  84.2 190.6 %reduce-scatter.10.cloned.1.call-done = bf16[1,128,128]{2,1,0:T(8,128)(2,1)} async-done(((bf16[32,128,128]{2,1,0:T(8,128)(2,1)}), bf16[1,128,128]{2,1,0:T(8,128)(2,1)}) %reduce-scatter.10.cloned.1.call-update) | async-done | bytes 32784 | tf_op jit(solution)/shard_map/reduce_scatter | solution.py:107
  274.9 1.4 bitcast_convert_fusion.2
  276.2 217.8 %reduce-scatter.14.cloned.1.call-done = bf16[1,128,128]{2,1,0:T(8,128)(2,1)} async-done(((bf16[32,128,128]{2,1,0:T(8,128)(2,1)}), bf16[1,128,128]{2,1,0:T(8,128)(2,1)}) %reduce-scatter.14.cloned.1.call-update) | async-done | bytes 32784 | tf_op jit(solution)/shard_map/reduce_scatter | solution.py:107
  494.0 1.4 bitcast_convert_fusion
  495.4 217.6 %reduce-scatter.12.cloned.1.call-done = bf16[1,128,128]{2,1,0:T(8,128)(2,1)} async-done(((bf16[32,128,128]{2,1,0:T(8,128)(2,1)}), bf16[1,128,128]{2,1,0:T(8,128)(2,1)}) %reduce-scatter.12.cloned.1.call-update) | async-done | bytes 32784 | tf_op jit(solution)/shard_map/reduce_scatter | solution.py:107
  713.0 1.4 bitcast_convert_fusion.1
  714.4 35.5 %reduce-scatter.6.cloned.1.call-done = bf16[128,512]{1,0:T(8,128)(2,1)} async-done(((bf16[128,4096]{1,0:T(8,128)(2,1)}), bf16[128,512]{1,0:T(8,128)(2,1)}) %reduce-scatter.6.cloned.1.call-update) | async-done | bytes 131088 | tf_op jit(solution)/shard_map/reduce_scatter | solution.py:83
  749.9 36.6 %reduce-scatter.8.cloned.1.call-done = bf16[128,512]{1,0:T(8,128)(2,1)} async-done(((bf16[128,4096]{1,0:T(8,128)(2,1)}), bf16[128,512]{1,0:T(8,128)(2,1)}) %reduce-scatter.8.cloned.1.call-update) | async-done | bytes 131088 | tf_op jit(solution)/shard_map/reduce_scatter | solution.py:112
  (30 shorter events, 0.1 us)
Async XLA Ops:
  7.2 27.7 %copy-start = (bf16[1,32,128,128]{3,2,1,0:T(8,128)(2,1)S(1)}, bf16[1,32,128,128]{3,2,1,0:T(8,128)(2,1)}, u32[]{:S(2)}) copy-start(bf16[1,32,128,128]{3,2,1,0:T(8,128)(2,1)} %param.19) | copy-start | bytes 3145732
  7.2 8.3 %copy-start.9 = (s32[1,32]{1,0:T(1,128)S(1)}, s32[1,32]{1,0:T(1,128)}, u32[]{:S(2)}) copy-start(s32[1,32]{1,0:T(1,128)} %param.14) | copy-start | bytes 388
  7.2 8.4 %copy-start.10 = (s32[1,32]{1,0:T(1,128)S(1)}, s32[1,32]{1,0:T(1,128)}, u32[]{:S(2)}) copy-start(s32[1,32]{1,0:T(1,128)} %param.16) | copy-start | bytes 388
  7.2 8.4 %copy-start.11 = (s32[1,32]{1,0:T(1,128)S(1)}, s32[1,32]{1,0:T(1,128)}, u32[]{:S(2)}) copy-start(s32[1,32]{1,0:T(1,128)} %param.18) | copy-start | bytes 388
  7.2 33.3 %all-gather.2.cloned.1.call-start = ((), (), s32[]{:S(2)}) async-start(), calls=%async_computation.6 | async-start | bytes 1179648 | tf_op jit(solution)/shard_map/all_gather | solution.py:56
  11.2 22.3 %all-to-all-start = ((bf16[128,8,512]{0,2,1:T(8,128)(2,1)}), bf16[128,8,512]{0,2,1:T(8,128)(2,1)S(1)}, u32[]{:S(2)}, u32[]{:S(2)}) async-start(bf16[128,8,512]{0,2,1:T(8,128)(2,1)} %tile.2), calls=%async_computation.1 | async-start | bytes 2097152 | tf_op jit(solution)/shard_map/all_to_all | solution.py:51
  15.5 259.4 %reduce-scatter.10.cloned.1.call-start = ((), (), s32[]{:S(2)}) async-start(), calls=%async_computation.9 | async-start | bytes 1081344 | tf_op jit(solution)/shard_map/reduce_scatter | solution.py:107
  34.8 1.0 copy-start.6
  42.1 3.3 copy-start.2
  47.2 2.3 copy-start.1
  47.2 2.3 copy-start.5
  50.0 2.3 copy-start.8
  58.2 435.9 %reduce-scatter.14.cloned.1.call-start = ((), (), s32[]{:S(2)}) async-start(), calls=%async_computation.11 | async-start | bytes 1081344 | tf_op jit(solution)/shard_map/reduce_scatter | solution.py:107
  63.3 649.7 %reduce-scatter.12.cloned.1.call-start = ((), (), s32[]{:S(2)}) async-start(), calls=%async_computation.10 | async-start | bytes 1081344 | tf_op jit(solution)/shard_map/reduce_scatter | solution.py:107
  65.0 3.4 copy-start.7
  68.4 681.5 %reduce-scatter.6.cloned.1.call-start = ((), (), s32[]{:S(2)}) async-start(), calls=%async_computation.7 | async-start | bytes 1179648 | tf_op jit(solution)/shard_map/reduce_scatter | solution.py:83
  73.4 2.3 copy-start.3
  73.4 713.0 %reduce-scatter.8.cloned.1.call-start = ((), (), s32[]{:S(2)}) async-start(), calls=%async_computation.8 | async-start | bytes 1179648 | tf_op jit(solution)/shard_map/reduce_scatter | solution.py:112
  73.4 2.3 copy-start.4
Sparse Core Ops, SparseCore 0:
  10.5 30.0 all-gather.1
  58.3 216.5 reduce-scatter.9
  278.7 215.3 reduce-scatter.13
  497.7 215.2 reduce-scatter.11
  715.9 33.8 reduce-scatter.5
  752.8 33.5 reduce-scatter.7
